TPU v7x, 512 devices: a whole 4x8x8 slice. The times are simulated.
512 devices in a mesh: feat: 16 (over x, z_hi, core), samp: 32 (over y, z_lo).
Axes of the slice: x: 4, y: 8, z: 8 (z_hi: 2, z_lo: 4; z = z_hi * 4 + z_lo), core: 2. Of those that a mesh axis runs over, the one named last changes fastest.
Arguments:
- tier_one: bfloat16 [8192, 12288], P('feat', 'samp')
- residuals: bfloat16 [12288, 128], P('samp'), may hold values from -6 to 6
- pair_list: int32 [3, 65536], P(None, 'feat'), may hold values from 0 to 8191, as said below
Outputs:
- scores: float32 [65536, 128], P(('feat', 'samp'))
Inputs may be any that keep to these rules, and one draw needn't show every extreme that they name: `pair_list`: rows 0 and 1 are feature indices, row 2 an operator id of 0 to 3; each descriptor's two features differ.
All inputs are finite; a program needn't handle non-finite values.
Results may differ from a plain program's by a relative error of at most 0.0031.
Values may be sent and summed in bfloat16 or wider, within the bound.
No kernel may reach another device: no remote copies, remote signals or barrier semaphores. Data moves between devices by JAX's collectives and lax.ppermute only.
A program may use at most 64 MiB of HBM per device.

v0:
```python
import math
import jax
import jax.numpy as jnp
import numpy as np
from jax import lax
from jax.sharding import Mesh
from jax.sharding import PartitionSpec as P

epsilon = 1e-05
FEAT_AXES = ("x", "zh", "c")
SAMP_AXES = ("y", "zl")
EXTRA_ROWS = 16


def combine_rows(first_rows, second_rows, operator_id):
    first_rows = first_rows.astype(jnp.float32)
    second_rows = second_rows.astype(jnp.float32)
    quotient = first_rows / (1.0 + jnp.abs(second_rows))
    built = jnp.where(
        operator_id == 0,
        first_rows + second_rows,
        jnp.where(
            operator_id == 1,
            first_rows - second_rows,
            jnp.where(operator_id == 2, first_rows * second_rows, quotient),
        ),
    )
    return built.astype(jnp.bfloat16)


def ring_gather(block, axis, n):
    assert n == 4
    fwd = [(i, (i + 1) % n) for i in range(n)]
    bwd = [(i, (i - 1) % n) for i in range(n)]
    from_left = lax.ppermute(block, axis, perm=fwd)
    from_right = lax.ppermute(block, axis, perm=bwd)
    half = block.shape[0] // 2
    far_a = lax.ppermute(from_left[:half], axis, perm=fwd)
    far_b = lax.ppermute(from_right[half:], axis, perm=bwd)
    return jnp.concatenate([block, from_right, far_a, far_b, from_left], axis=0)


def split3(v):
    hi = lax.reduce_precision(v, exponent_bits=8, mantissa_bits=7)
    rest = v - hi
    mid = lax.reduce_precision(rest, exponent_bits=8, mantissa_bits=7)
    lo = rest - mid
    return jnp.stack([hi, mid, lo], axis=-2).astype(jnp.bfloat16)


def finish(product, first_sums, square_sums, col_totals, sample_count):
    means = first_sums / sample_count
    variance = square_sums / sample_count - means * means
    centred = product - means[:, None] * col_totals[None, :]
    return centred * lax.rsqrt(variance + epsilon)[:, None] / math.sqrt(sample_count)


def per_device(tier_one, residuals, pair_list):
    local_rows = tier_one.shape[0]
    local_pairs = pair_list.shape[1]
    width_k = residuals.shape[1]
    n_x = lax.axis_size("x")
    n_zh = lax.axis_size("zh")
    n_y = lax.axis_size("y")
    n_zl = lax.axis_size("zl")
    n_samp = n_y * n_zl
    sample_count = residuals.shape[0] * n_samp
    rows = lax.all_gather(tier_one, "zh", axis=0, tiled=True)
    rows = ring_gather(rows, "x", n_x)
    other = lax.ppermute(rows, "c", perm=[(0, 1), (1, 0)])
    rows = jnp.concatenate([rows, other], axis=0)
    my_c = lax.axis_index("c")
    my_x = lax.axis_index("x")

    def position(g):
        f, r = (g // local_rows, g % local_rows)
        x, zh, c = (f // (2 * n_zh), f // 2 % n_zh, f % 2)
        half = (c != my_c).astype(jnp.int32)
        x_slot = (x - my_x + n_x) % n_x
        return ((half * n_x + x_slot) * n_zh + zh) * local_rows + r

    first = jnp.take(rows, position(pair_list[0]), axis=0)
    second = jnp.take(rows, position(pair_list[1]), axis=0)
    built = combine_rows(first, second, pair_list[2][:, None])
    product = jnp.dot(built, residuals, preferred_element_type=jnp.float32)
    widened = built.astype(jnp.float32)
    first_sums = jnp.sum(widened, axis=1)
    square_sums = jnp.sum(widened * widened, axis=1)
    col_part = jnp.sum(residuals.astype(jnp.float32), axis=0)
    local_samples = residuals.shape[0]
    local_means = first_sums / local_samples
    centred = product - local_means[:, None] * col_part[None, :]
    blocks = local_pairs // width_k
    block_rows = width_k + EXTRA_ROWS
    extras = jnp.concatenate(
        [
            split3(jnp.broadcast_to(col_part[None, :], (blocks, width_k))),
            split3(first_sums.reshape(blocks, width_k)),
            split3(square_sums.reshape(blocks, width_k)),
            jnp.zeros((blocks, EXTRA_ROWS - 9, width_k), jnp.bfloat16),
        ],
        axis=1,
    )
    packed = jnp.concatenate(
        [centred.astype(jnp.bfloat16).reshape(blocks, width_k, width_k), extras], axis=1
    )
    arrived = lax.all_to_all(packed, SAMP_AXES, 0, 0, tiled=False)
    centred_sum = jnp.sum(arrived[:, :width_k].astype(jnp.float32), axis=0)
    pieces = arrived[:, width_k:].astype(jnp.float32)

    def joined(i):
        return pieces[:, i] + pieces[:, i + 1] + pieces[:, i + 2]

    col_parts, first_parts, square_parts = (joined(0), joined(3), joined(6))
    mean_share = jnp.einsum(
        "dp,dk->pk", first_parts / local_samples, col_parts, precision=lax.Precision.HIGHEST
    )
    return finish(
        centred_sum + mean_share,
        jnp.sum(first_parts, axis=0),
        jnp.sum(square_parts, axis=0),
        jnp.sum(col_parts, axis=0),
        sample_count,
    )


def solution(mesh):
    n_feat, n_samp = mesh.devices.shape
    n_c, n_zh = (2, 2)
    n_x = n_feat // (n_c * n_zh)
    n_zl = 4
    n_y = n_samp // n_zl
    devices = np.asarray(mesh.devices).reshape(n_x, n_zh, n_c, n_y, n_zl)
    fine = Mesh(devices, FEAT_AXES + SAMP_AXES)
    in_specs = (P(FEAT_AXES, SAMP_AXES), P(SAMP_AXES, None), P(None, FEAT_AXES))
    out_specs = P(FEAT_AXES + SAMP_AXES, None)
    return jax.shard_map(
        per_device, mesh=fine, in_specs=in_specs, out_specs=out_specs, check_vma=False
    )
```

profile of v0, /device:TPU:6, one launch (start us, length us, event | category | flops | bytes accessed | tf_op | source)
XLA Modules:
  0.0 170.4 jit_solution(11472657003874128858)
XLA Ops:
  0.0 19.2 %all_gather.3 = bf16[1024,384]{1,0:T(8,128)(2,1)S(1)} all-gather(bf16[512,384]{1,0:T(8,128)(2,1)} %param.5), channel_id=1, replica_groups=mesh['x'=4,'zh'=2,'c'=2,'y'=8,'zl'=4] {'zh'}, dimensions={0}, use_global_device_ids=true | all-gather | bytes 1179648 | tf_op jit(solution)/shard_map/all_gather | solution.py:68
  19.2 2.4 %collective-permute-start.1 = (bf16[1024,384]{1,0:T(8,128)(2,1)S(1)}, bf16[1024,384]{1,0:T(8,128)(2,1)S(1)}, u32[]{:S(2)}, u32[]{:S(2)}) collective-permute-start(bf16[1024,384]{1,0:T(8,128)(2,1)S(1)} %all_gather.3), channel_id=1, source_target_pairs={{0,128},{128,256},{256,384},{384,0},{1,129},{129,257},{257,385},{3... | collective-permute-start | bytes 2359304 | tf_op jit(solution)/shard_map/ppermute | solution.py:35
  21.6 3.5 %collective-permute-start = (bf16[1024,384]{1,0:T(8,128)(2,1)S(1)}, bf16[1024,384]{1,0:T(8,128)(2,1)S(1)}, u32[]{:S(2)}, u32[]{:S(2)}) collective-permute-start(bf16[1024,384]{1,0:T(8,128)(2,1)S(1)} %all_gather.3), channel_id=1, source_target_pairs={{0,384},{128,0},{256,128},{384,256},{1,385},{129,1},{257,129},{385... | collective-permute-start | bytes 2359304 | tf_op jit(solution)/shard_map/ppermute | solution.py:36
  25.0 14.7 %collective-permute-done.1 = bf16[1024,384]{1,0:T(8,128)(2,1)S(1)} collective-permute-done((bf16[1024,384]{1,0:T(8,128)(2,1)S(1)}, bf16[1024,384]{1,0:T(8,128)(2,1)S(1)}, u32[]{:S(2)}, u32[]{:S(2)}) %collective-permute-start.1) | collective-permute-done | bytes 786464 | tf_op jit(solution)/shard_map/ppermute | solution.py:35
  39.8 3.4 %collective-permute-start.2 = (bf16[512,384]{1,0:T(8,128)(2,1)S(1)}, bf16[512,384]{1,0:T(8,128)(2,1)S(1)}, u32[]{:S(2)}, u32[]{:S(2)}) collective-permute-start(bf16[512,384]{1,0:T(8,128)(2,1)S(1)} %slice.68), channel_id=1, source_target_pairs={{0,128},{128,256},{256,384},{384,0},{1,129},{129,257},{257,385},{3... | collective-permute-start | bytes 1179656 | tf_op jit(solution)/shard_map/ppermute | solution.py:38
  43.2 0.0 collective-permute-done
  43.3 2.4 %collective-permute-start.3 = (bf16[512,384]{1,0:T(8,128)(2,1)S(1)}, bf16[512,384]{1,0:T(8,128)(2,1)S(1)}, u32[]{:S(2)}, u32[]{:S(2)}) collective-permute-start(bf16[512,384]{1,0:T(8,128)(2,1)S(1)} %slice.69), channel_id=1, source_target_pairs={{0,384},{128,0},{256,128},{384,256},{1,385},{129,1},{257,129},{385... | collective-permute-start | bytes 1179656 | tf_op jit(solution)/shard_map/ppermute | solution.py:39
  45.7 1.3 constant_dynamic-update-slice_fusion.4
  47.0 0.0 copy-start
  47.0 1.3 constant_dynamic-update-slice_fusion.3
  48.3 2.7 %collective-permute-done.2 = bf16[512,384]{1,0:T(8,128)(2,1)S(1)} collective-permute-done((bf16[512,384]{1,0:T(8,128)(2,1)S(1)}, bf16[512,384]{1,0:T(8,128)(2,1)S(1)}, u32[]{:S(2)}, u32[]{:S(2)}) %collective-permute-start.2) | collective-permute-done | bytes 393248 | tf_op jit(solution)/shard_map/ppermute | solution.py:38
  51.0 1.0 constant_dynamic-update-slice_fusion.2
  52.0 3.2 %collective-permute-done.3 = bf16[512,384]{1,0:T(8,128)(2,1)S(1)} collective-permute-done((bf16[512,384]{1,0:T(8,128)(2,1)S(1)}, bf16[512,384]{1,0:T(8,128)(2,1)S(1)}, u32[]{:S(2)}, u32[]{:S(2)}) %collective-permute-start.3) | collective-permute-done | bytes 393248 | tf_op jit(solution)/shard_map/ppermute | solution.py:39
  55.2 1.0 constant_dynamic-update-slice_fusion.1
  56.3 1.3 constant_dynamic-update-slice_fusion
  57.6 1.9 %collective-permute-start.4 = (bf16[4096,384]{1,0:T(8,128)(2,1)}, bf16[4096,384]{1,0:T(8,128)(2,1)S(1)}, u32[]{:S(2)}, u32[]{:S(2)}) collective-permute-start(bf16[4096,384]{1,0:T(8,128)(2,1)} %get-tuple-element.20), channel_id=1, source_target_pairs={{0,32},{32,0},{1,33},{33,1},{2,34},{34,2},{3,35},{35,3},{4,36},{36... | collective-permute-start | bytes 9437192 | tf_op jit(solution)/shard_map/ppermute | solution.py:70
  59.5 0.0 copy-done
  59.5 0.1 convert_reduce_fusion.2
  59.6 0.0 copy-done.1
  59.6 0.2 compare_reduce_fusion.2
  59.8 0.1 compare_and_fusion
  60.0 5.4 %collective-permute-done.4 = bf16[4096,384]{1,0:T(8,128)(2,1)S(1)} collective-permute-done((bf16[4096,384]{1,0:T(8,128)(2,1)}, bf16[4096,384]{1,0:T(8,128)(2,1)S(1)}, u32[]{:S(2)}, u32[]{:S(2)}) %collective-permute-start.4) | collective-permute-done | bytes 3145760 | tf_op jit(solution)/shard_map/ppermute | solution.py:70
  65.4 2.0 %constant_dynamic-update-slice_fusion.5 = bf16[8192,384]{1,0:T(8,128)(2,1)} fusion(bf16[8192,384]{1,0:T(8,128)(2,1)} %get-tuple-element.21, bf16[4096,384]{1,0:T(8,128)(2,1)S(1)} %collective-permute-done.4), kind=kLoop, calls=%fused_computation.80 | loop fusion | bytes 6291456 | tf_op jit(solution)/shard_map/concatenate | solution.py:71
  67.4 17.6 %gather_fusion = bf16[4096,384]{1,0:T(8,128)(2,1)S(1)} fusion(bf16[8192,384]{1,0:T(8,128)(2,1)} %constant_dynamic-update-slice_fusion.5, s32[4096]{0:T(1024)S(1)} %broadcast_clamp_fusion.1), kind=kCustom, calls=%fused_computation.clone | custom fusion | bytes 6307840 | tf_op jit(solution)/shard_map/jit(_take)/gather | solution.py:82
  85.0 20.3 %gather_fusion.1 = bf16[4096,384]{1,0:T(8,128)(2,1)} fusion(bf16[8192,384]{1,0:T(8,128)(2,1)} %constant_dynamic-update-slice_fusion.5, s32[4096]{0:T(1024)S(1)} %broadcast_clamp_fusion), kind=kCustom, calls=%fused_computation.1.clone | custom fusion | bytes 6307840 | tf_op jit(solution)/shard_map/jit(_take)/gather | solution.py:83
  105.3 8.6 %fusion = (f32[4096]{0:T(1024)S(1)}, f32[4096]{0:T(1024)S(1)}, bf16[4096,384]{1,0:T(8,128)(2,1)S(1)}) fusion(pred[4096]{0:T(1024)(128)(4,1)S(1)} %get-tuple-element.10, pred[4096]{0:T(1024)(128)(4,1)S(1)} %get-tuple-element.9, bf16[4096,384]{1,0:T(8,128)(2,1)} %gather_fusion.1, pred[4096]{0:T(1024)(128)(4,1)S(1)} %get-tuple-element.18, ...), kind=kLoop, calls=%fused_computation.9 | loop fusion | flops 28303360 | bytes 9490432 | tf_op jit(solution)/shard_map/reduce_sum | solution.py:88
  114.1 1.2 fusion.6
  115.4 0.6 concatenate.13
  116.0 53.1 %all_to_all.5 = bf16[32,144,128]{2,1,0:T(8,128)(2,1)S(1)} all-to-all(bf16[32,144,128]{2,1,0:T(8,128)(2,1)S(1)} %concatenate.13), channel_id=1, replica_groups=mesh['x'=4,'zh'=2,'c'=2,'y'=8,'zl'=4] {'y','zl'}, dimensions={0} | all-to-all | bytes 2359296 | tf_op jit(solution)/shard_map/all_to_all | solution.py:107
  169.1 0.1 fusion.42
  169.3 0.2 convert_reduce_fusion.1
  169.5 0.9 fusion.9
  (23 shorter events, 0.3 us)
Async XLA Ops:
  19.2 20.6 %collective-permute-start.1 = (bf16[1024,384]{1,0:T(8,128)(2,1)S(1)}, bf16[1024,384]{1,0:T(8,128)(2,1)S(1)}, u32[]{:S(2)}, u32[]{:S(2)}) collective-permute-start(bf16[1024,384]{1,0:T(8,128)(2,1)S(1)} %all_gather.3), channel_id=1, source_target_pairs={{0,128},{128,256},{256,384},{384,0},{1,129},{129,257},{257,385},{3... | collective-permute-start | bytes 2359304 | tf_op jit(solution)/shard_map/ppermute | solution.py:35
  21.6 21.6 %collective-permute-start = (bf16[1024,384]{1,0:T(8,128)(2,1)S(1)}, bf16[1024,384]{1,0:T(8,128)(2,1)S(1)}, u32[]{:S(2)}, u32[]{:S(2)}) collective-permute-start(bf16[1024,384]{1,0:T(8,128)(2,1)S(1)} %all_gather.3), channel_id=1, source_target_pairs={{0,384},{128,0},{256,128},{384,256},{1,385},{129,1},{257,129},{385... | collective-permute-start | bytes 2359304 | tf_op jit(solution)/shard_map/ppermute | solution.py:36
  39.8 11.2 %collective-permute-start.2 = (bf16[512,384]{1,0:T(8,128)(2,1)S(1)}, bf16[512,384]{1,0:T(8,128)(2,1)S(1)}, u32[]{:S(2)}, u32[]{:S(2)}) collective-permute-start(bf16[512,384]{1,0:T(8,128)(2,1)S(1)} %slice.68), channel_id=1, source_target_pairs={{0,128},{128,256},{256,384},{384,0},{1,129},{129,257},{257,385},{3... | collective-permute-start | bytes 1179656 | tf_op jit(solution)/shard_map/ppermute | solution.py:38
  43.3 12.0 %collective-permute-start.3 = (bf16[512,384]{1,0:T(8,128)(2,1)S(1)}, bf16[512,384]{1,0:T(8,128)(2,1)S(1)}, u32[]{:S(2)}, u32[]{:S(2)}) collective-permute-start(bf16[512,384]{1,0:T(8,128)(2,1)S(1)} %slice.69), channel_id=1, source_target_pairs={{0,384},{128,0},{256,128},{384,256},{1,385},{129,1},{257,129},{385... | collective-permute-start | bytes 1179656 | tf_op jit(solution)/shard_map/ppermute | solution.py:39
  47.0 12.5 %copy-start = (bf16[384,128]{1,0:T(8,128)(2,1)S(1)}, bf16[384,128]{1,0:T(8,128)(2,1)}, u32[]{:S(2)}) copy-start(bf16[384,128]{1,0:T(8,128)(2,1)} %param.6) | copy-start | bytes 294916
  47.0 12.6 %copy-start.1 = (s32[3,4096]{1,0:T(4,128)S(1)}, s32[3,4096]{1,0:T(4,128)}, u32[]{:S(2)}) copy-start(s32[3,4096]{1,0:T(4,128)} %param.7) | copy-start | bytes 147460
  57.6 7.8 %collective-permute-start.4 = (bf16[4096,384]{1,0:T(8,128)(2,1)}, bf16[4096,384]{1,0:T(8,128)(2,1)S(1)}, u32[]{:S(2)}, u32[]{:S(2)}) collective-permute-start(bf16[4096,384]{1,0:T(8,128)(2,1)} %get-tuple-element.20), channel_id=1, source_target_pairs={{0,32},{32,0},{1,33},{33,1},{2,34},{34,2},{3,35},{35,3},{4,36},{36... | collective-permute-start | bytes 9437192 | tf_op jit(solution)/shard_map/ppermute | solution.py:70
where the time goes:
time: 171 us; the launch traced here: 170 us
  blocking collectives  72.3 us (42%)
  local copies, waits for them, and re-layouts  46.7 us (27%)
  waiting for transfers between devices  26.1 us (15%)
  starting transfers between devices  13.6 us (8%)
  other arithmetic  9.33 us (5%)
  matrix products  2.11 us (1%)
    all_to_all x1, blocking collectives, per_device(): arrived = lax.all_to_all(packed, SAMP_AXES, 0, 0, tiled=False)  53.1 us
    gather x1, local copies, waits for them, and re-layouts, per_device(): second = jnp.take(rows, position(pair_list[1]), axis=0)  20.3 us
    all_gather x1, blocking collectives, per_device(): rows = lax.all_gather(tier_one, 'zh', axis=0, tiled=True)  19.2 us
    gather x1, local copies, waits for them, and re-layouts, per_device(): first = jnp.take(rows, position(pair_list[0]), axis=0)  17.6 us
    ppermute x1, waiting for transfers between devices, ring_gather(): from_left = lax.ppermute(block, axis, perm=fwd)  14.7 us
    reduce_sum x1, other arithmetic, per_device(): square_sums = jnp.sum(widened * widened, axis=1)  8.61 us
    ppermute x1, waiting for transfers between devices, per_device(): other = lax.ppermute(rows, 'c', perm=[(0, 1), (1, 0)])  5.39 us
    unnamed x8, local copies, waits for them, and re-layouts  4.57 us
  transfers between devices with their start and end apart: 5, of which 4 were waited for; matrix products, arithmetic and copies ran while one was open for 2% of the time, Pallas kernels for 0%

commit v1 on v0

--- a/solution.py
+++ b/solution.py
@@ -65,7 +65,8 @@
     n_zl = lax.axis_size("zl")
     n_samp = n_y * n_zl
     sample_count = residuals.shape[0] * n_samp
-    rows = lax.all_gather(tier_one, "zh", axis=0, tiled=True)
+    stack = jnp.stack([tier_one] * lax.axis_size("zh"))
+    rows = jnp.concatenate(lax.all_to_all(stack, "zh", 0, 0), axis=0)
     rows = ring_gather(rows, "x", n_x)
     other = lax.ppermute(rows, "c", perm=[(0, 1), (1, 0)])
     rows = jnp.concatenate([rows, other], axis=0)

time: 171 us -> 178 us (1.041)
  blocking collectives: 72.3 us -> 81.3 us
  waiting for transfers between devices: 26.1 us -> 22.7 us
    all_to_all x0 -> x1, blocking collectives: none -> 33.2 us  [per_device(): rows = jnp.concatenate(lax.all_to_all(stack, 'zh', 0, 0), axis=0)]
    all_gather x1 -> x0, blocking collectives: 19.2 us -> none  [per_device(): rows = lax.all_gather(tier_one, 'zh', axis=0, tiled=True)]
    all_to_all x1, blocking collectives: 53.1 us -> 48.1 us  [per_device(): arrived = lax.all_to_all(packed, SAMP_AXES, 0, 0, tiled=False)]
    ppermute x1, waiting for transfers between devices: 14.7 us -> 12.2 us  [ring_gather(): from_left = lax.ppermute(block, axis, perm=fwd)]
where the time goes in v1:
time: 178 us; the launch traced here: 177 us
  blocking collectives  81.3 us (46%)
  local copies, waits for them, and re-layouts  46.7 us (26%)
  waiting for transfers between devices  22.7 us (13%)
  starting transfers between devices  13.6 us (8%)
  other arithmetic  10.6 us (6%)
  matrix products  2.12 us (1%)
    all_to_all x1, blocking collectives, per_device(): arrived = lax.all_to_all(packed, SAMP_AXES, 0, 0, tiled=False)  48.1 us
    all_to_all x1, blocking collectives, per_device(): rows = jnp.concatenate(lax.all_to_all(stack, 'zh', 0, 0), axis=0)  33.2 us
    gather x1, local copies, waits for them, and re-layouts, per_device(): second = jnp.take(rows, position(pair_list[1]), axis=0)  20.3 us
    gather x1, local copies, waits for them, and re-layouts, per_device(): first = jnp.take(rows, position(pair_list[0]), axis=0)  17.6 us
    ppermute x1, waiting for transfers between devices, ring_gather(): from_left = lax.ppermute(block, axis, perm=fwd)  12.2 us
    reduce_sum x1, other arithmetic, per_device(): square_sums = jnp.sum(widened * widened, axis=1)  8.61 us
    ppermute x1, waiting for transfers between devices, per_device(): other = lax.ppermute(rows, 'c', perm=[(0, 1), (1, 0)])  5.39 us
    unnamed x8, local copies, waits for them, and re-layouts  4.57 us
  transfers between devices with their start and end apart: 5, of which 4 were waited for; matrix products, arithmetic and copies ran while one was open for 2% of the time, Pallas kernels for 0%

profile of v1, /device:TPU:6, one launch (start us, length us, event | category | flops | bytes accessed | tf_op | source)
XLA Modules:
  0.0 177.3 jit_solution(853915937602880994)
XLA Ops:
  0.0 1.2 pad_maximum_fusion
  1.2 33.2 %all_to_all.10 = bf16[2,512,384]{2,1,0:T(8,128)(2,1)S(1)} all-to-all(bf16[2,512,384]{2,1,0:T(8,128)(2,1)S(1)} %pad_maximum_fusion), channel_id=1, replica_groups=mesh['x'=4,'zh'=2,'c'=2,'y'=8,'zl'=4] {'zh'}, dimensions={0} | all-to-all | bytes 1572864 | tf_op jit(solution)/shard_map/all_to_all | solution.py:69
  34.4 2.4 %collective-permute-start.1 = (bf16[1024,384]{1,0:T(8,128)(2,1)S(1)}, bf16[1024,384]{1,0:T(8,128)(2,1)S(1)}, u32[]{:S(2)}, u32[]{:S(2)}) collective-permute-start(bf16[1024,384]{1,0:T(8,128)(2,1)S(1)} %bitcast.25), channel_id=1, source_target_pairs={{0,128},{128,256},{256,384},{384,0},{1,129},{129,257},{257,385},{3... | collective-permute-start | bytes 2359304 | tf_op jit(solution)/shard_map/ppermute | solution.py:35
  36.8 3.5 %collective-permute-start = (bf16[1024,384]{1,0:T(8,128)(2,1)S(1)}, bf16[1024,384]{1,0:T(8,128)(2,1)S(1)}, u32[]{:S(2)}, u32[]{:S(2)}) collective-permute-start(bf16[1024,384]{1,0:T(8,128)(2,1)S(1)} %bitcast.26), channel_id=1, source_target_pairs={{0,384},{128,0},{256,128},{384,256},{1,385},{129,1},{257,129},{385... | collective-permute-start | bytes 2359304 | tf_op jit(solution)/shard_map/ppermute | solution.py:36
  40.3 12.2 %collective-permute-done.1 = bf16[1024,384]{1,0:T(8,128)(2,1)S(1)} collective-permute-done((bf16[1024,384]{1,0:T(8,128)(2,1)S(1)}, bf16[1024,384]{1,0:T(8,128)(2,1)S(1)}, u32[]{:S(2)}, u32[]{:S(2)}) %collective-permute-start.1) | collective-permute-done | bytes 786464 | tf_op jit(solution)/shard_map/ppermute | solution.py:35
  52.6 3.6 %collective-permute-start.2 = (bf16[512,384]{1,0:T(8,128)(2,1)S(1)}, bf16[512,384]{1,0:T(8,128)(2,1)S(1)}, u32[]{:S(2)}, u32[]{:S(2)}) collective-permute-start(bf16[512,384]{1,0:T(8,128)(2,1)S(1)} %slice.68), channel_id=1, source_target_pairs={{0,128},{128,256},{256,384},{384,0},{1,129},{129,257},{257,385},{3... | collective-permute-start | bytes 1179656 | tf_op jit(solution)/shard_map/ppermute | solution.py:38
  56.2 0.0 collective-permute-done
  56.2 2.2 %collective-permute-start.3 = (bf16[512,384]{1,0:T(8,128)(2,1)S(1)}, bf16[512,384]{1,0:T(8,128)(2,1)S(1)}, u32[]{:S(2)}, u32[]{:S(2)}) collective-permute-start(bf16[512,384]{1,0:T(8,128)(2,1)S(1)} %slice.69), channel_id=1, source_target_pairs={{0,384},{128,0},{256,128},{384,256},{1,385},{129,1},{257,129},{385... | collective-permute-start | bytes 1179656 | tf_op jit(solution)/shard_map/ppermute | solution.py:39
  58.5 1.3 constant_dynamic-update-slice_fusion.4
  59.8 1.3 constant_dynamic-update-slice_fusion.3
  61.1 1.2 collective-permute-done.2
  62.2 1.0 constant_dynamic-update-slice_fusion.2
  63.2 3.9 %collective-permute-done.3 = bf16[512,384]{1,0:T(8,128)(2,1)S(1)} collective-permute-done((bf16[512,384]{1,0:T(8,128)(2,1)S(1)}, bf16[512,384]{1,0:T(8,128)(2,1)S(1)}, u32[]{:S(2)}, u32[]{:S(2)}) %collective-permute-start.3) | collective-permute-done | bytes 393248 | tf_op jit(solution)/shard_map/ppermute | solution.py:39
  67.1 1.0 constant_dynamic-update-slice_fusion.1
  68.1 1.3 constant_dynamic-update-slice_fusion
  69.5 1.9 %collective-permute-start.4 = (bf16[4096,384]{1,0:T(8,128)(2,1)}, bf16[4096,384]{1,0:T(8,128)(2,1)S(1)}, u32[]{:S(2)}, u32[]{:S(2)}) collective-permute-start(bf16[4096,384]{1,0:T(8,128)(2,1)} %get-tuple-element.20), channel_id=1, source_target_pairs={{0,32},{32,0},{1,33},{33,1},{2,34},{34,2},{3,35},{35,3},{4,36},{36... | collective-permute-start | bytes 9437192 | tf_op jit(solution)/shard_map/ppermute | solution.py:71
  71.4 0.0 copy-done
  71.4 0.1 convert_reduce_fusion.2
  71.5 0.0 copy-done.1
  71.5 0.2 compare_reduce_fusion.2
  71.7 0.1 compare_and_fusion
  71.8 5.4 %collective-permute-done.4 = bf16[4096,384]{1,0:T(8,128)(2,1)S(1)} collective-permute-done((bf16[4096,384]{1,0:T(8,128)(2,1)}, bf16[4096,384]{1,0:T(8,128)(2,1)S(1)}, u32[]{:S(2)}, u32[]{:S(2)}) %collective-permute-start.4) | collective-permute-done | bytes 3145760 | tf_op jit(solution)/shard_map/ppermute | solution.py:71
  77.2 2.0 %constant_dynamic-update-slice_fusion.5 = bf16[8192,384]{1,0:T(8,128)(2,1)} fusion(bf16[8192,384]{1,0:T(8,128)(2,1)} %get-tuple-element.21, bf16[4096,384]{1,0:T(8,128)(2,1)S(1)} %collective-permute-done.4), kind=kLoop, calls=%fused_computation.81 | loop fusion | bytes 6291456 | tf_op jit(solution)/shard_map/concatenate | solution.py:72
  79.2 17.6 %gather_fusion = bf16[4096,384]{1,0:T(8,128)(2,1)S(1)} fusion(bf16[8192,384]{1,0:T(8,128)(2,1)} %constant_dynamic-update-slice_fusion.5, s32[4096]{0:T(1024)S(1)} %broadcast_clamp_fusion.1), kind=kCustom, calls=%fused_computation.clone | custom fusion | bytes 6307840 | tf_op jit(solution)/shard_map/jit(_take)/gather | solution.py:83
  96.9 20.3 %gather_fusion.1 = bf16[4096,384]{1,0:T(8,128)(2,1)} fusion(bf16[8192,384]{1,0:T(8,128)(2,1)} %constant_dynamic-update-slice_fusion.5, s32[4096]{0:T(1024)S(1)} %broadcast_clamp_fusion), kind=kCustom, calls=%fused_computation.1.clone | custom fusion | bytes 6307840 | tf_op jit(solution)/shard_map/jit(_take)/gather | solution.py:84
  117.2 8.6 %fusion = (f32[4096]{0:T(1024)S(1)}, f32[4096]{0:T(1024)S(1)}, bf16[4096,384]{1,0:T(8,128)(2,1)S(1)}) fusion(pred[4096]{0:T(1024)(128)(4,1)S(1)} %get-tuple-element.10, pred[4096]{0:T(1024)(128)(4,1)S(1)} %get-tuple-element.9, bf16[4096,384]{1,0:T(8,128)(2,1)} %gather_fusion.1, pred[4096]{0:T(1024)(128)(4,1)S(1)} %get-tuple-element.18, ...), kind=kLoop, calls=%fused_computation.9 | loop fusion | flops 28303360 | bytes 9490432 | tf_op jit(solution)/shard_map/reduce_sum | solution.py:89
  126.0 1.2 fusion.6
  127.2 0.6 concatenate.13
  127.9 48.1 %all_to_all.11 = bf16[32,144,128]{2,1,0:T(8,128)(2,1)S(1)} all-to-all(bf16[32,144,128]{2,1,0:T(8,128)(2,1)S(1)} %concatenate.13), channel_id=1, replica_groups=mesh['x'=4,'zh'=2,'c'=2,'y'=8,'zl'=4] {'y','zl'}, dimensions={0} | all-to-all | bytes 2359296 | tf_op jit(solution)/shard_map/all_to_all | solution.py:108
  176.0 0.1 fusion.42
  176.2 0.2 convert_reduce_fusion.1
  176.3 0.9 fusion.9
  (24 shorter events, 0.3 us)
Async XLA Ops:
  34.4 18.1 %collective-permute-start.1 = (bf16[1024,384]{1,0:T(8,128)(2,1)S(1)}, bf16[1024,384]{1,0:T(8,128)(2,1)S(1)}, u32[]{:S(2)}, u32[]{:S(2)}) collective-permute-start(bf16[1024,384]{1,0:T(8,128)(2,1)S(1)} %bitcast.25), channel_id=1, source_target_pairs={{0,128},{128,256},{256,384},{384,0},{1,129},{129,257},{257,385},{3... | collective-permute-start | bytes 2359304 | tf_op jit(solution)/shard_map/ppermute | solution.py:35
  36.8 19.4 %collective-permute-start = (bf16[1024,384]{1,0:T(8,128)(2,1)S(1)}, bf16[1024,384]{1,0:T(8,128)(2,1)S(1)}, u32[]{:S(2)}, u32[]{:S(2)}) collective-permute-start(bf16[1024,384]{1,0:T(8,128)(2,1)S(1)} %bitcast.26), channel_id=1, source_target_pairs={{0,384},{128,0},{256,128},{384,256},{1,385},{129,1},{257,129},{385... | collective-permute-start | bytes 2359304 | tf_op jit(solution)/shard_map/ppermute | solution.py:36
  52.6 9.7 %collective-permute-start.2 = (bf16[512,384]{1,0:T(8,128)(2,1)S(1)}, bf16[512,384]{1,0:T(8,128)(2,1)S(1)}, u32[]{:S(2)}, u32[]{:S(2)}) collective-permute-start(bf16[512,384]{1,0:T(8,128)(2,1)S(1)} %slice.68), channel_id=1, source_target_pairs={{0,128},{128,256},{256,384},{384,0},{1,129},{129,257},{257,385},{3... | collective-permute-start | bytes 1179656 | tf_op jit(solution)/shard_map/ppermute | solution.py:38
  56.2 10.9 %collective-permute-start.3 = (bf16[512,384]{1,0:T(8,128)(2,1)S(1)}, bf16[512,384]{1,0:T(8,128)(2,1)S(1)}, u32[]{:S(2)}, u32[]{:S(2)}) collective-permute-start(bf16[512,384]{1,0:T(8,128)(2,1)S(1)} %slice.69), channel_id=1, source_target_pairs={{0,384},{128,0},{256,128},{384,256},{1,385},{129,1},{257,129},{385... | collective-permute-start | bytes 1179656 | tf_op jit(solution)/shard_map/ppermute | solution.py:39
  59.8 11.6 %copy-start = (bf16[384,128]{1,0:T(8,128)(2,1)S(1)}, bf16[384,128]{1,0:T(8,128)(2,1)}, u32[]{:S(2)}) copy-start(bf16[384,128]{1,0:T(8,128)(2,1)} %param.6) | copy-start | bytes 294916
  59.8 11.7 %copy-start.1 = (s32[3,4096]{1,0:T(4,128)S(1)}, s32[3,4096]{1,0:T(4,128)}, u32[]{:S(2)}) copy-start(s32[3,4096]{1,0:T(4,128)} %param.7) | copy-start | bytes 147460
  69.5 7.8 %collective-permute-start.4 = (bf16[4096,384]{1,0:T(8,128)(2,1)}, bf16[4096,384]{1,0:T(8,128)(2,1)S(1)}, u32[]{:S(2)}, u32[]{:S(2)}) collective-permute-start(bf16[4096,384]{1,0:T(8,128)(2,1)} %get-tuple-element.20), channel_id=1, source_target_pairs={{0,32},{32,0},{1,33},{33,1},{2,34},{34,2},{3,35},{35,3},{4,36},{36... | collective-permute-start | bytes 9437192 | tf_op jit(solution)/shard_map/ppermute | solution.py:71
